TPU v7x, 256 devices: a whole 4x4x8 slice. The times are simulated.
256 devices in a mesh: ctx: 32 (over x, y, core), tp: 8 (over z).
Axes of the slice: x: 4, y: 4, z: 8, core: 2. Of those that a mesh axis runs over, the one named last changes fastest.
Arguments:
- tokens: bfloat16 [8192, 4096], P('ctx'), may hold values from -700 to 700
- doc_lengths: int32 [64], replicated, may hold values from 1 to 4096, 8192 in all
- norm_gain: bfloat16 [4096], replicated, may hold values from 0.099609375 to 1.8984375
- w_query: bfloat16 [4096, 4096], P(None, 'tp'), may hold values from -3 to 3
- w_key: bfloat16 [4096, 1024], P(None, 'tp'), may hold values from -3 to 3
- w_value: bfloat16 [4096, 1024], P(None, 'tp'), may hold values from -0.09375 to 0.09375
- w_out: bfloat16 [4096, 4096], P('tp'), may hold values from -0.5 to 0.5
Outputs:
- mixed: bfloat16 [8192, 4096], P('ctx', 'tp')
Inputs may be any that keep to these rules, and one draw needn't show every extreme that they name: `doc_lengths`: document lengths in packing order; they sum to 8192, and the longest has exactly 4096 tokens.
All inputs are finite; a program needn't handle non-finite values.
Results may differ from a plain program's by a relative error of at most 0.02.
The roundings to bfloat16 on the way count: a program that leaves them out, or rounds other values in their place, can miss the bound.
Values may be sent and summed in bfloat16 or wider, within the bound.
No kernel may reach another device: no remote copies, remote signals or barrier semaphores. Data moves between devices by JAX's collectives and lax.ppermute only.
A program may use at most 64 MiB of HBM per device.

v0:
```python
import jax
import jax.numpy as jnp
from jax import lax
from jax.sharding import PartitionSpec as P

HEAD_DIM = 128


NEGATIVE = -1e30
ROPE_BASE = 500000.0
EPSILON = 1e-05


def doc_starts(doc_lengths):
    ends = jnp.cumsum(doc_lengths)
    return ends - doc_lengths


def seg_info(positions, starts):
    inside = starts[None, :] <= positions[:, None]
    segment = jnp.sum(inside.astype(jnp.int32), axis=1) - 1
    doc_first = jnp.max(jnp.where(inside, starts[None, :], 0), axis=1)
    return (segment, doc_first)


def rotate(lifted, offsets):
    halfway = lifted.shape[-1] // 2
    fraction = jnp.arange(halfway, dtype=jnp.float32) * (2.0 / lifted.shape[-1])
    inverse = jnp.exp(-jnp.log(jnp.float32(ROPE_BASE)) * fraction)
    angles = offsets.astype(jnp.float32)[:, None] * inverse[None, :]
    cosine = jnp.cos(angles)[:, None, :]
    sine_table = jnp.sin(angles)[:, None, :]
    leading = lifted[..., :halfway]
    trailing = lifted[..., halfway:]
    return jnp.concatenate(
        [leading * cosine - trailing * sine_table, trailing * cosine + leading * sine_table],
        axis=-1,
    )


def normalize(tokens, norm_gain):
    widened = tokens.astype(jnp.float32)
    square = jnp.mean(widened * widened, axis=-1, keepdims=True)
    return (widened * lax.rsqrt(square + EPSILON) * norm_gain.astype(jnp.float32)).astype(
        jnp.bfloat16
    )


def project(normed, weight, offsets):
    head_count = weight.shape[1] // HEAD_DIM
    lifted = jnp.dot(normed, weight, preferred_element_type=jnp.float32)
    lifted = lifted.reshape(normed.shape[0], head_count, HEAD_DIM)
    return rotate(lifted, offsets).astype(jnp.bfloat16)


def block_terms(query_block, key_block, value_block, allowed):
    scores = jnp.einsum(
        "tkgd,skd->kgts", query_block, key_block, preferred_element_type=jnp.float32
    ) * HEAD_DIM ** (-0.5)
    scores = jnp.where(allowed[None, None], scores, NEGATIVE)
    highest = jnp.max(scores, axis=-1)
    weights = jnp.where(allowed[None, None], jnp.exp(scores - highest[..., None]), 0.0).astype(
        jnp.bfloat16
    )
    numerator = jnp.einsum(
        "kgts,skd->tkgd", weights, value_block, preferred_element_type=jnp.float32
    )
    denominator = jnp.sum(weights.astype(jnp.float32), axis=-1)
    return (highest, numerator, denominator)


def combine(carried, terms):
    highest, numerator, denominator = carried
    block_high, block_num, block_den = terms
    summit = jnp.maximum(highest, block_high)
    retain = jnp.exp(highest - summit)
    admit = jnp.exp(block_high - summit)
    numerator = (
        numerator * jnp.transpose(retain, (2, 0, 1))[..., None]
        + block_num * jnp.transpose(admit, (2, 0, 1))[..., None]
    )
    denominator = denominator * retain + block_den * admit
    return (summit, numerator, denominator)


def finish(carried):
    numerator = carried[1]
    denominator = jnp.transpose(carried[2], (2, 0, 1))[..., None]
    result = (numerator / denominator).astype(jnp.bfloat16)
    return result.reshape(numerator.shape[0], -1)


def on_device(tokens, doc_lengths, norm_gain, w_query, w_key, w_value, w_out):
    shard_rows = tokens.shape[0]
    heads_here = w_query.shape[1] // HEAD_DIM
    pairs_here = w_key.shape[1] // HEAD_DIM
    sharing = heads_here // pairs_here
    ctx_count = lax.axis_size("ctx")
    ctx_place = lax.axis_index("ctx")
    starts = doc_starts(doc_lengths)
    local_places = jnp.arange(shard_rows, dtype=jnp.int32)
    positions = ctx_place * shard_rows + local_places
    segment, doc_first = seg_info(positions, starts)
    lowest = doc_first[0]
    normed = normalize(tokens, norm_gain)
    offsets = positions - doc_first
    queries = project(normed, w_query, offsets).reshape(shard_rows, pairs_here, sharing, HEAD_DIM)
    keys = project(normed, w_key, offsets).reshape(shard_rows, pairs_here * HEAD_DIM)
    values = jnp.dot(normed, w_value, preferred_element_type=jnp.float32).astype(jnp.bfloat16)
    packed = jnp.stack([keys, values])

    def absorb(carried, kv_pair, block_index, query_set, query_places, query_segments):
        key_places = block_index * shard_rows + local_places
        key_segments, unused_first = seg_info(key_places, starts)
        allowed = (key_segments[None, :] == query_segments[:, None]) & (
            key_places[None, :] <= query_places[:, None]
        )
        key_block = kv_pair[0].reshape(shard_rows, pairs_here, HEAD_DIM)
        value_block = kv_pair[1].reshape(shard_rows, pairs_here, HEAD_DIM)
        return combine(carried, block_terms(query_set, key_block, value_block, allowed))

    def consider(carried, kv_pair, block_index, query_set, query_places, query_segments, ranges):
        block_end = block_index * shard_rows + shard_rows - 1
        useful = jnp.zeros((), jnp.bool_)
        for range_low, range_high in ranges:
            useful = useful | (block_index * shard_rows <= range_high) & (block_end >= range_low)
        useful = useful & (block_index >= 0)
        return lax.cond(
            useful,
            lambda state: absorb(
                state, kv_pair, block_index, query_set, query_places, query_segments
            ),
            lambda state: state,
            carried,
        )

    initial = (
        jnp.full((pairs_here, sharing, shard_rows), NEGATIVE, jnp.float32),
        jnp.zeros((shard_rows, pairs_here, sharing, HEAD_DIM), jnp.float32),
        jnp.zeros((pairs_here, sharing, shard_rows), jnp.float32),
    )
    own_ranges = ((lowest, positions[shard_rows - 1]),)
    gathered = lax.all_gather(packed, "ctx", axis=1, tiled=True)
    blocks_per_turn = max(1, ctx_count // 16)

    def one_turn(turn_index, carried):
        for within in range(blocks_per_turn):
            block_index = turn_index * blocks_per_turn + within
            kv_pair = lax.dynamic_slice_in_dim(gathered, block_index * shard_rows, shard_rows, 1)
            carried = consider(
                carried, kv_pair, block_index, queries, positions, segment, own_ranges
            )
        return carried

    attended = finish(lax.fori_loop(0, ctx_count // blocks_per_turn, one_turn, initial))
    partial_value = jnp.dot(attended, w_out, preferred_element_type=jnp.float32)
    summed = lax.psum_scatter(
        partial_value.astype(jnp.bfloat16), "tp", scatter_dimension=1, tiled=True
    )
    return summed


def solution(mesh):
    placed = (P("ctx", None), P(), P(), P(None, "tp"), P(None, "tp"), P(None, "tp"), P("tp", None))
    return jax.shard_map(
        on_device, mesh=mesh, in_specs=placed, out_specs=P("ctx", "tp"), check_vma=False
    )
```

profile of v0, /device:TPU:28, one launch (start us, length us, event | category | flops | bytes accessed | tf_op | source)
XLA Modules:
  0.0 260.2 jit_solution(4132926780315079240)
XLA Ops:
  6.6 2.2 fusion.30
  11.3 2.6 fusion.33
  17.1 4.3 %fusion.48 = f32[256,512]{1,0:T(8,128)} fusion(bf16[4096,512]{1,0:T(8,128)(2,1)} %param.16, bf16[256,4096]{1,0:T(8,128)(2,1)S(1)} %copy-done.1, f32[4096]{0:T(1024)S(1)} %convert_element_type.97, f32[256]{0:T(256)S(1)} %add_rsqrt_fusion), kind=kOutput, calls=%fused_computation.96 | convolution fusion | flops 1077936128 | bytes 6833152 | tf_op jit(solution)/shard_map/dot_general | solution.py:51
  21.4 1.2 reshape.426
  23.8 46.5 %all-gather.2.cloned.1.call-done = bf16[2,8192,128]{1,2,0:T(8,128)(2,1)} async-done(((bf16[2,256,128]{1,2,0:T(8,128)(2,1)}), bf16[2,8192,128]{1,2,0:T(8,128)(2,1)}) %all-gather.2.cloned.1.call-update) | async-done | bytes 4194320 | tf_op jit(solution)/shard_map/all_gather | solution.py:143
  70.3 6.4 %copy.43 = bf16[2,8192,128]{2,1,0:T(8,128)(2,1)} copy(bf16[2,8192,128]{1,2,0:T(8,128)(2,1)} %all-gather.2.cloned.1.call-done) | data formatting | bytes 8388608
  76.7 102.2 %while.24 = (s32[]{:T(128)}, f32[1,4,256]{2,1,0:T(4,128)S(1)}, f32[256,1,4,128]{0,3,2,1:T(8,128)S(1)}, f32[1,4,256]{2,1,0:T(4,128)S(1)}, s32[]{:T(128)}, /*index...) while((s32[]{:T(128)}, f32[1,4,256]{2,1,0:T(4,128)S(1)}, ...), condition=%wide.region_15.16_spmd.clone.clone, body=%wide.region_4.15_spmd.clone.clone.sunk | while | flops 275493632 | bytes 13024521 | solution.py:155
  99.9 5.3 %conditional.8 = (f32[1,4,256]{2,1,0:T(4,128)S(1)}, f32[256,1,4,128]{3,0,2,1:T(8,128)}, f32[1,4,256]{2,1,0:T(4,128)S(1)}, f32[256,1,4,128]{0,3,2,1:T(8,128)S(1)}) conditional(s32[]{:T(128)} %convert_element_type.154, (f32[1,4,256]{2,1,0:T(4,128)S(1)}, f32[256,1,4,128]{0,3,2,1:T(8,128)S(1)}, f32[1,4,256]{2,1,0:T(4,128)S(1)}) %tuple.115, ...), branch_computations={%region_5.5_spmd, %region_6.9_spmd.clone} | conditional | flops 137746688 | bytes 7035242 | solution.py:128
  100.4 1.2 fusion.53
  101.8 2.2 fusion.20
  104.0 1.2 copy.52
  105.2 4.2 %conditional.9 = ((f32[1,4,256]{2,1,0:T(4,128)S(1)}, f32[256,1,4,128]{0,3,2,1:T(8,128)S(1)}, f32[1,4,256]{2,1,0:T(4,128)S(1)})) conditional(s32[]{:T(128)} %convert_element_type.153, (f32[1,4,256]{2,1,0:T(4,128)S(1)}, f32[256,1,4,128]{0,3,2,1:T(8,128)S(1)}, f32[1,4,256]{2,1,0:T(4,128)S(1)}) %tuple.117, (s32[64]{0:T(128)S(1)}, s32[]{:T(128)}, ...), branch_computations={%region_10.10_spmd, %region_11.14_spmd} | conditional | flops 137746688 | bytes 5986666 | solution.py:128
  105.5 1.2 copy.38
  108.2 1.2 fusion.7
  111.8 5.3 %conditional.8 = (f32[1,4,256]{2,1,0:T(4,128)S(1)}, f32[256,1,4,128]{3,0,2,1:T(8,128)}, f32[1,4,256]{2,1,0:T(4,128)S(1)}, f32[256,1,4,128]{0,3,2,1:T(8,128)S(1)}) conditional(s32[]{:T(128)} %convert_element_type.154, (f32[1,4,256]{2,1,0:T(4,128)S(1)}, f32[256,1,4,128]{0,3,2,1:T(8,128)S(1)}, f32[1,4,256]{2,1,0:T(4,128)S(1)}) %tuple.115, ...), branch_computations={%region_5.5_spmd, %region_6.9_spmd.clone} | conditional | flops 137746688 | bytes 7035242 | solution.py:128
  112.3 1.2 fusion.53
  113.8 2.2 fusion.20
  115.9 1.2 copy.52
  117.2 4.2 %conditional.9 = ((f32[1,4,256]{2,1,0:T(4,128)S(1)}, f32[256,1,4,128]{0,3,2,1:T(8,128)S(1)}, f32[1,4,256]{2,1,0:T(4,128)S(1)})) conditional(s32[]{:T(128)} %convert_element_type.153, (f32[1,4,256]{2,1,0:T(4,128)S(1)}, f32[256,1,4,128]{0,3,2,1:T(8,128)S(1)}, f32[1,4,256]{2,1,0:T(4,128)S(1)}) %tuple.117, (s32[64]{0:T(128)S(1)}, s32[]{:T(128)}, ...), branch_computations={%region_10.10_spmd, %region_11.14_spmd} | conditional | flops 137746688 | bytes 5986666 | solution.py:128
  117.5 1.2 copy.38
  118.7 1.2 fusion.52
  120.2 1.2 fusion.7
  123.8 5.3 %conditional.8 = (f32[1,4,256]{2,1,0:T(4,128)S(1)}, f32[256,1,4,128]{3,0,2,1:T(8,128)}, f32[1,4,256]{2,1,0:T(4,128)S(1)}, f32[256,1,4,128]{0,3,2,1:T(8,128)S(1)}) conditional(s32[]{:T(128)} %convert_element_type.154, (f32[1,4,256]{2,1,0:T(4,128)S(1)}, f32[256,1,4,128]{0,3,2,1:T(8,128)S(1)}, f32[1,4,256]{2,1,0:T(4,128)S(1)}) %tuple.115, ...), branch_computations={%region_5.5_spmd, %region_6.9_spmd.clone} | conditional | flops 137746688 | bytes 7035242 | solution.py:128
  125.7 2.2 fusion.20
  127.9 1.2 copy.52
  129.1 4.2 %conditional.9 = ((f32[1,4,256]{2,1,0:T(4,128)S(1)}, f32[256,1,4,128]{0,3,2,1:T(8,128)S(1)}, f32[1,4,256]{2,1,0:T(4,128)S(1)})) conditional(s32[]{:T(128)} %convert_element_type.153, (f32[1,4,256]{2,1,0:T(4,128)S(1)}, f32[256,1,4,128]{0,3,2,1:T(8,128)S(1)}, f32[1,4,256]{2,1,0:T(4,128)S(1)}) %tuple.117, (s32[64]{0:T(128)S(1)}, s32[]{:T(128)}, ...), branch_computations={%region_10.10_spmd, %region_11.14_spmd} | conditional | flops 137746688 | bytes 5986666 | solution.py:128
  129.4 1.2 copy.38
  130.7 1.2 fusion.52
  132.1 1.2 fusion.7
  135.8 5.3 %conditional.8 = (f32[1,4,256]{2,1,0:T(4,128)S(1)}, f32[256,1,4,128]{3,0,2,1:T(8,128)}, f32[1,4,256]{2,1,0:T(4,128)S(1)}, f32[256,1,4,128]{0,3,2,1:T(8,128)S(1)}) conditional(s32[]{:T(128)} %convert_element_type.154, (f32[1,4,256]{2,1,0:T(4,128)S(1)}, f32[256,1,4,128]{0,3,2,1:T(8,128)S(1)}, f32[1,4,256]{2,1,0:T(4,128)S(1)}) %tuple.115, ...), branch_computations={%region_5.5_spmd, %region_6.9_spmd.clone} | conditional | flops 137746688 | bytes 7035242 | solution.py:128
  136.3 1.2 fusion.53
  137.7 2.2 fusion.20
  139.9 1.2 copy.52
  141.1 4.2 %conditional.9 = ((f32[1,4,256]{2,1,0:T(4,128)S(1)}, f32[256,1,4,128]{0,3,2,1:T(8,128)S(1)}, f32[1,4,256]{2,1,0:T(4,128)S(1)})) conditional(s32[]{:T(128)} %convert_element_type.153, (f32[1,4,256]{2,1,0:T(4,128)S(1)}, f32[256,1,4,128]{0,3,2,1:T(8,128)S(1)}, f32[1,4,256]{2,1,0:T(4,128)S(1)}) %tuple.117, (s32[64]{0:T(128)S(1)}, s32[]{:T(128)}, ...), branch_computations={%region_10.10_spmd, %region_11.14_spmd} | conditional | flops 137746688 | bytes 5986666 | solution.py:128
  141.4 1.2 copy.38
  144.1 1.2 fusion.7
  147.7 5.3 %conditional.8 = (f32[1,4,256]{2,1,0:T(4,128)S(1)}, f32[256,1,4,128]{3,0,2,1:T(8,128)}, f32[1,4,256]{2,1,0:T(4,128)S(1)}, f32[256,1,4,128]{0,3,2,1:T(8,128)S(1)}) conditional(s32[]{:T(128)} %convert_element_type.154, (f32[1,4,256]{2,1,0:T(4,128)S(1)}, f32[256,1,4,128]{0,3,2,1:T(8,128)S(1)}, f32[1,4,256]{2,1,0:T(4,128)S(1)}) %tuple.115, ...), branch_computations={%region_5.5_spmd, %region_6.9_spmd.clone} | conditional | flops 137746688 | bytes 7035242 | solution.py:128
  148.2 1.2 fusion.53
  149.7 2.2 fusion.20
  151.8 1.2 copy.52
  153.1 4.2 %conditional.9 = ((f32[1,4,256]{2,1,0:T(4,128)S(1)}, f32[256,1,4,128]{0,3,2,1:T(8,128)S(1)}, f32[1,4,256]{2,1,0:T(4,128)S(1)})) conditional(s32[]{:T(128)} %convert_element_type.153, (f32[1,4,256]{2,1,0:T(4,128)S(1)}, f32[256,1,4,128]{0,3,2,1:T(8,128)S(1)}, f32[1,4,256]{2,1,0:T(4,128)S(1)}) %tuple.117, (s32[64]{0:T(128)S(1)}, s32[]{:T(128)}, ...), branch_computations={%region_10.10_spmd, %region_11.14_spmd} | conditional | flops 137746688 | bytes 5986666 | solution.py:128
  153.4 1.2 copy.38
  156.0 1.2 fusion.7
  159.7 5.3 %conditional.8 = (f32[1,4,256]{2,1,0:T(4,128)S(1)}, f32[256,1,4,128]{3,0,2,1:T(8,128)}, f32[1,4,256]{2,1,0:T(4,128)S(1)}, f32[256,1,4,128]{0,3,2,1:T(8,128)S(1)}) conditional(s32[]{:T(128)} %convert_element_type.154, (f32[1,4,256]{2,1,0:T(4,128)S(1)}, f32[256,1,4,128]{0,3,2,1:T(8,128)S(1)}, f32[1,4,256]{2,1,0:T(4,128)S(1)}) %tuple.115, ...), branch_computations={%region_5.5_spmd, %region_6.9_spmd.clone} | conditional | flops 137746688 | bytes 7035242 | solution.py:128
  161.6 2.2 fusion.20
  163.8 1.2 copy.52
  178.9 4.8 %convolution_convert_fusion = bf16[256,4096]{1,0:T(8,128)(2,1)} fusion(bf16[256,512]{0,1:T(8,128)(2,1)S(1)} %bitcast.145, bf16[512,4096]{1,0:T(8,128)(2,1)} %param.19), kind=kOutput, calls=%fused_computation.59 | convolution fusion | flops 1074790400 | bytes 6553600 | tf_op jit(solution)/shard_map/dot_general | solution.py:156
  183.8 69.5 %reduce-scatter.2.cloned.1.call-done = bf16[256,512]{1,0:T(8,128)(2,1)} async-done(((bf16[256,4096]{1,0:T(8,128)(2,1)}), bf16[256,512]{1,0:T(8,128)(2,1)}) %reduce-scatter.2.cloned.1.call-update) | async-done | bytes 262160 | tf_op jit(solution)/shard_map/reduce_scatter | solution.py:157
  (196 shorter events, 39.4 us)
Async XLA Ops:
  6.5 4.8 %copy-start = (bf16[4096,128]{1,0:T(8,128)(2,1)S(1)}, bf16[4096,128]{1,0:T(8,128)(2,1)}, u32[]{:S(2)}) copy-start(bf16[4096,128]{1,0:T(8,128)(2,1)} %param.18) | copy-start | bytes 3145732
  6.5 7.4 %copy-start.1 = (bf16[256,4096]{1,0:T(8,128)(2,1)S(1)}, bf16[256,4096]{1,0:T(8,128)(2,1)}, u32[]{:S(2)}) copy-start(bf16[256,4096]{1,0:T(8,128)(2,1)} %param.13) | copy-start | bytes 6291460
  6.5 63.8 %all-gather.2.cloned.1.call-start = ((), (), s32[]{:S(2)}) async-start(), calls=%async_computation.1 | async-start | bytes 4325376 | tf_op jit(solution)/shard_map/all_gather | solution.py:143
  10.5 3.5 %copy-start.2 = (bf16[4096,128]{1,0:T(8,128)(2,1)S(1)}, bf16[4096,128]{1,0:T(8,128)(2,1)}, u32[]{:S(2)}) copy-start(bf16[4096,128]{1,0:T(8,128)(2,1)} %param.17) | copy-start | bytes 3145732
  15.9 237.4 %reduce-scatter.2.cloned.1.call-start = ((), (), s32[]{:S(2)}) async-start(), calls=%async_computation.2 | async-start | bytes 2359296 | tf_op jit(solution)/shard_map/reduce_scatter | solution.py:157
Sparse Core Ops, SparseCore 0:
  16.1 54.2 all-gather.1
  183.9 69.3 reduce-scatter.1
where the time goes:
time: 264 us; the launch traced here: 260 us
  waiting for transfers between devices  116 us (44%)
  matrix products  44.4 us (17%)
  loops' own time  40.2 us (15%)
  local copies, waits for them, and re-layouts  34.6 us (13%)
  between operations  13.5 us (5%)
  other arithmetic  11.3 us (4%)
    reduce_scatter x1, waiting for transfers between devices, on_device(): lax.psum_scatter(partial_value.astype(jnp.bfloat16), 'tp', scatter_dimens...  69.5 us
    all_gather x1, waiting for transfers between devices, on_device(): gathered = lax.all_gather(packed, 'ctx', axis=1, tiled=True)  46.5 us
    another operation x1, loops' own time, on_device(): lax.fori_loop(0, ctx_count // blocks_per_turn, one_turn, initial)  39.1 us
    dot_general x11, matrix products, block_terms(): jnp.einsum('kgts,skd->tkgd', weights, value_block, preferred_element_type...  19 us
    another operation x22, local copies, waits for them, and re-layouts  18 us
    dot_general x11, matrix products, block_terms(): jnp.einsum('tkgd,skd->kgts', query_block, key_block, preferred_element_ty...  12.8 us
    cond x6, local copies, waits for them, and re-layouts, consider(): lax.cond(useful, lambda state: absorb(state, kv_pair, block_index, query_...  7.41 us
    unnamed x7, local copies, waits for them, and re-layouts  6.38 us
  transfers between devices with their start and end apart: 2, of which 2 were waited for; matrix products, arithmetic and copies ran while one was open for 3% of the time, Pallas kernels for 0%

commit v1 on v0

v1 whole, which is shorter than its diff:
```python
import functools

import jax
import jax.numpy as jnp
from jax import lax
from jax.experimental import pallas as pl
from jax.experimental.pallas import tpu as pltpu
from jax.sharding import PartitionSpec as P

HEAD_DIM = 128
MOST = 4096


NEGATIVE = -1e30
ROPE_BASE = 500000.0
EPSILON = 1e-05


def doc_starts(doc_lengths):
    ends = jnp.cumsum(doc_lengths)
    return ends - doc_lengths


def seg_info(positions, starts):
    inside = starts[None, :] <= positions[:, None]
    segment = jnp.sum(inside.astype(jnp.int32), axis=1) - 1
    doc_first = jnp.max(jnp.where(inside, starts[None, :], 0), axis=1)
    return (segment, doc_first)


def rotate(lifted, offsets):
    halfway = lifted.shape[-1] // 2
    fraction = jnp.arange(halfway, dtype=jnp.float32) * (2.0 / lifted.shape[-1])
    inverse = jnp.exp(-jnp.log(jnp.float32(ROPE_BASE)) * fraction)
    angles = offsets.astype(jnp.float32)[:, None] * inverse[None, :]
    cosine = jnp.cos(angles)[:, None, :]
    sine_table = jnp.sin(angles)[:, None, :]
    leading = lifted[..., :halfway]
    trailing = lifted[..., halfway:]
    return jnp.concatenate(
        [leading * cosine - trailing * sine_table, trailing * cosine + leading * sine_table],
        axis=-1,
    )


def normalize(tokens, norm_gain):
    widened = tokens.astype(jnp.float32)
    square = jnp.mean(widened * widened, axis=-1, keepdims=True)
    return (widened * lax.rsqrt(square + EPSILON) * norm_gain.astype(jnp.float32)).astype(
        jnp.bfloat16
    )


def project(normed, weight, offsets):
    head_count = weight.shape[1] // HEAD_DIM
    lifted = jnp.dot(normed, weight, preferred_element_type=jnp.float32)
    lifted = lifted.reshape(normed.shape[0], head_count, HEAD_DIM)
    return rotate(lifted, offsets).astype(jnp.bfloat16)


def flash_kernel(bounds, q_ref, kv_ref, kseg_ref, qseg_ref, o_ref, m_sc, l_sc, acc_sc, *, heads):
    step = pl.program_id(0)
    first = bounds[0]
    own = bounds[1]
    block = first + step
    rows = q_ref.shape[0]

    @pl.when(step == 0)
    def _():
        m_sc[...] = jnp.full(m_sc.shape, NEGATIVE, jnp.float32)
        l_sc[...] = jnp.zeros(l_sc.shape, jnp.float32)
        acc_sc[...] = jnp.zeros(acc_sc.shape, jnp.float32)

    @pl.when(block <= own)
    def _():
        keys = kv_ref[0]
        values = kv_ref[1]
        query_places = own * rows + lax.broadcasted_iota(jnp.int32, (rows, rows), 0)
        key_places = block * rows + lax.broadcasted_iota(jnp.int32, (rows, rows), 1)
        allowed = (qseg_ref[...] == kseg_ref[...]) & (key_places <= query_places)
        for h in range(heads):
            query = q_ref[:, h * HEAD_DIM:(h + 1) * HEAD_DIM]
            scores = lax.dot_general(
                query, keys, (((1,), (1,)), ((), ())), preferred_element_type=jnp.float32
            ) * HEAD_DIM ** (-0.5)
            scores = jnp.where(allowed, scores, NEGATIVE)
            highest = jnp.max(scores, axis=1, keepdims=True)
            weights = jnp.where(allowed, jnp.exp(scores - highest), 0.0).astype(jnp.bfloat16)
            numerator = jnp.dot(weights, values, preferred_element_type=jnp.float32)
            denominator = jnp.sum(weights.astype(jnp.float32), axis=1, keepdims=True)
            previous = m_sc[h]
            summit = jnp.maximum(previous, highest)
            retain = jnp.exp(previous - summit)
            admit = jnp.exp(highest - summit)
            acc_sc[h] = acc_sc[h] * retain + numerator * admit
            l_sc[h] = l_sc[h] * retain + denominator * admit
            m_sc[h] = summit

    @pl.when(step == pl.num_programs(0) - 1)
    def _():
        for h in range(heads):
            o_ref[:, h * HEAD_DIM:(h + 1) * HEAD_DIM] = (acc_sc[h] / l_sc[h]).astype(o_ref.dtype)


def flash(bounds, queries, gathered, key_segments, query_segments, steps):
    rows, width = queries.shape
    heads = width // HEAD_DIM

    def kv_map(step, b):
        return (0, jnp.minimum(b[0] + step, b[1]), 0)

    def kseg_map(step, b):
        return (0, jnp.minimum(b[0] + step, b[1]))

    grid_spec = pltpu.PrefetchScalarGridSpec(
        num_scalar_prefetch=1,
        grid=(steps,),
        in_specs=[
            pl.BlockSpec((rows, width), lambda step, b: (0, 0)),
            pl.BlockSpec((2, rows, HEAD_DIM), kv_map),
            pl.BlockSpec((1, rows), kseg_map),
            pl.BlockSpec((rows, 1), lambda step, b: (0, 0)),
        ],
        out_specs=pl.BlockSpec((rows, width), lambda step, b: (0, 0)),
        scratch_shapes=[
            pltpu.VMEM((heads, rows, 1), jnp.float32),
            pltpu.VMEM((heads, rows, 1), jnp.float32),
            pltpu.VMEM((heads, rows, HEAD_DIM), jnp.float32),
        ],
    )
    return pl.pallas_call(
        functools.partial(flash_kernel, heads=heads),
        grid_spec=grid_spec,
        out_shape=jax.ShapeDtypeStruct((rows, width), jnp.bfloat16),
    )(bounds, queries, gathered, key_segments, query_segments)


def on_device(tokens, doc_lengths, norm_gain, w_query, w_key, w_value, w_out):
    shard_rows = tokens.shape[0]
    ctx_count = lax.axis_size("ctx")
    ctx_place = lax.axis_index("ctx")
    starts = doc_starts(doc_lengths)
    local_places = jnp.arange(shard_rows, dtype=jnp.int32)
    positions = ctx_place * shard_rows + local_places
    segment, doc_first = seg_info(positions, starts)
    every_place = jnp.arange(shard_rows * ctx_count, dtype=jnp.int32)
    every_segment, unused_first = seg_info(every_place, starts)
    normed = normalize(tokens, norm_gain)
    offsets = positions - doc_first
    queries = project(normed, w_query, offsets).reshape(shard_rows, -1)
    keys = project(normed, w_key, offsets).reshape(shard_rows, -1)
    values = jnp.dot(normed, w_value, preferred_element_type=jnp.float32).astype(jnp.bfloat16)
    packed = jnp.stack([keys, values])
    gathered = lax.all_gather(packed, "ctx", axis=1, tiled=True)
    bounds = jnp.stack([doc_first[0] // shard_rows, ctx_place]).astype(jnp.int32)
    steps = min(ctx_count, -(-(MOST - 1) // shard_rows) + 1)
    attended = flash(
        bounds,
        queries,
        gathered,
        every_segment.reshape(1, -1).astype(jnp.int32),
        segment.reshape(-1, 1).astype(jnp.int32),
        steps,
    )
    partial_value = jnp.dot(attended, w_out, preferred_element_type=jnp.float32)
    summed = lax.psum_scatter(
        partial_value.astype(jnp.bfloat16), "tp", scatter_dimension=1, tiled=True
    )
    return summed


def solution(mesh):
    placed = (P("ctx", None), P(), P(), P(None, "tp"), P(None, "tp"), P(None, "tp"), P("tp", None))
    return jax.shard_map(
        on_device, mesh=mesh, in_specs=placed, out_specs=P("ctx", "tp"), check_vma=False
    )
```

time: 264 us -> 169 us (0.64); the launches traced: 260 us -> 169 us
  loops' own time: 40.2 us -> 0 us
  matrix products: 44.4 us -> 12.5 us
  local copies, waits for them, and re-layouts: 34.6 us -> 4.17 us
  Pallas kernels: 0 us -> 8.58 us
  waiting for transfers between devices: 116 us -> 120 us
  other arithmetic: 11.3 us -> 8.13 us
    another operation x33 -> x0, loops' own time: 40.2 us -> none  [the longest x1 39.1 us: on_device(): lax.fori_loop(0, ctx_count // blocks_per_turn, one_turn, initial)]
    dot_general x22 -> x0, matrix products: 31.8 us -> none  [the longest x11 19 us: block_terms(): jnp.einsum('kgts,skd->tkgd', weights, value_block, preferred_element_type...]
    another operation x22 -> x1, local copies, waits for them, and re-layouts: 18 us -> 0.9 us
    reduce_scatter x1, waiting for transfers between devices: 69.5 us -> 80.9 us  [on_device(): lax.psum_scatter(partial_value.astype(jnp.bfloat16), 'tp', scatter_dimens...]
    pallas_call x0 -> x1, Pallas kernels: none -> 8.58 us  [flash(): pl.pallas_call(functools.partial(flash_kernel, heads=heads), grid_spec=gr...]
    all_gather x1, waiting for transfers between devices: 46.5 us -> 38.8 us  [on_device(): gathered = lax.all_gather(packed, 'ctx', axis=1, tiled=True)]
    cond x17 -> x0, local copies, waits for them, and re-layouts: 7.44 us -> none  [the longest x6 7.41 us: consider(): lax.cond(useful, lambda state: absorb(state, kv_pair, block_index, query_...]
    unnamed x7, local copies, waits for them, and re-layouts: 6.38 us -> 0.76 us
  transfers between devices with their start and end apart: 2 -> 2, of which waited for: 2 -> 2; matrix products, arithmetic and copies ran while one was open for 3% -> 6% of each run, Pallas kernels for 0% -> 0%
where the time goes in v1:
time: 169 us
  waiting for transfers between devices  120 us (71%)
  between operations  16.1 us (10%)
  matrix products  12.5 us (7%)
  Pallas kernels  8.58 us (5%)
  other arithmetic  8.13 us (5%)
  local copies, waits for them, and re-layouts  4.17 us (2%)
    reduce_scatter x1, waiting for transfers between devices, on_device(): lax.psum_scatter(partial_value.astype(jnp.bfloat16), 'tp', scatter_dimens...  80.9 us
    all_gather x1, waiting for transfers between devices, on_device(): gathered = lax.all_gather(packed, 'ctx', axis=1, tiled=True)  38.8 us
    pallas_call x1, Pallas kernels, flash(): pl.pallas_call(functools.partial(flash_kernel, heads=heads), grid_spec=gr...  8.58 us
    dot_general x2, matrix products, project(): lifted = jnp.dot(normed, weight, preferred_element_type=jnp.float32)  6.73 us
    dot_general x1, matrix products, on_device(): partial_value = jnp.dot(attended, w_out, preferred_element_type=jnp.float32)  4.89 us
  transfers between devices with their start and end apart: 2, of which 2 were waited for; matrix products, arithmetic and copies ran while one was open for 6% of the time, Pallas kernels for 0%

profile of v1, /device:TPU:28, one launch (start us, length us, event | category | flops | bytes accessed | tf_op | source)
XLA Modules:
  0.0 169.2 jit_solution(6245618283936900767)
XLA Ops:
  6.5 0.0 copy-start
  6.5 0.0 copy-start.1
  6.5 0.0 all-gather.2.cloned.1.call-start
  6.6 0.9 copy.13
  7.5 0.1 reduce-window.9
  7.6 0.1 reduce
  7.7 0.0 copy-start.2
  7.7 0.7 sub.32
  8.4 0.7 convert_element_type.45
  9.1 2.1 %fusion = f32[256]{0:T(256)S(1)} fusion(bf16[256,4096]{1,0:T(8,128)(2,1)} %param.7), kind=kLoop, calls=%fused_computation.3 | loop fusion | flops 3145472 | bytes 2098176 | tf_op jit(solution)/shard_map/reduce_sum | solution.py:48
  11.2 0.0 copy-done
  11.2 2.4 %convolution_bitcast_fusion = f32[256,1,128]{2,0,1:T(8,128)S(1)} fusion(bf16[4096,128]{1,0:T(8,128)(2,1)S(1)} %copy-done, bf16[256,4096]{1,0:T(8,128)(2,1)} %param.7, f32[4096]{0:T(1024)S(1)} %convert_element_type.45, f32[256]{0:T(256)S(1)} %add_rsqrt_fusion), kind=kOutput, calls=%fused_computation.8 | convolution fusion | flops 272629760 | bytes 3294208 | tf_op jit(solution)/shard_map/dot_general | solution.py:56
  13.7 0.0 copy-done.1
  13.7 0.0 copy-done.2
  13.7 0.9 fusion.3
  14.5 0.1 fusion.13
  14.6 0.6 fusion.15
  15.2 0.7 pad_maximum_fusion.1
  16.0 0.0 all-gather.2.cloned.1.call-update
  16.0 0.0 reduce-scatter.2.cloned.1.call-start
  16.0 0.5 slice.15
  19.2 4.3 %fusion.18 = f32[256,512]{1,0:T(8,128)} fusion(bf16[4096,512]{1,0:T(8,128)(2,1)} %param.10, bf16[256,4096]{1,0:T(8,128)(2,1)S(1)} %copy-done.1, f32[4096]{0:T(1024)S(1)} %convert_element_type.45, f32[256]{0:T(256)S(1)} %add_rsqrt_fusion), kind=kOutput, calls=%fused_computation.41 | convolution fusion | flops 1077936128 | bytes 6833152 | tf_op jit(solution)/shard_map/dot_general | solution.py:56
  23.5 1.2 reshape.215
  24.7 0.5 multiply_cosine_fusion.1
  25.2 0.5 subtract_convert_fusion
  25.7 0.4 pad_maximum_fusion
  26.1 0.7 copy.19
  26.9 0.8 copy.15.qseg_ref
  27.7 0.6 pad_add_fusion.bounds
  28.2 0.3 convert_reduce_fusion
  28.6 0.6 broadcast_add_fusion
  29.2 38.8 %all-gather.2.cloned.1.call-done.kv_ref = bf16[2,8192,128]{2,1,0:T(8,128)(2,1)} async-done(((bf16[2,256,128]{2,1,0:T(8,128)(2,1)}), bf16[2,8192,128]{2,1,0:T(8,128)(2,1)}) %all-gather.2.cloned.1.call-update) | async-done | bytes 4194320 | tf_op jit(solution)/shard_map/all_gather | solution.py:154
  68.0 8.6 %shard_map.73 = bf16[256,512]{1,0:T(8,128)(2,1)} custom-call(s32[2]{0:T(128)} %pad_add_fusion.bounds, bf16[256,512]{1,0:T(8,128)(2,1)} %bitcast.23, bf16[2,8192,128]{2,1,0:T(8,128)(2,1)} %all-gather.2.cloned.1.call-done.kv_ref, s32[1,8192]{1,0:T(1,128)} %bitcast.25, s32[256,1]{1,0:T(8,128)} %copy.15.qseg_ref), custom_call_target="tpu_custom_call" | custom-call | tf_op jit(solution)/shard_map/pallas_call | solution.py:131
  76.6 4.9 %convolution_convert_fusion = bf16[256,4096]{1,0:T(8,128)(2,1)} fusion(bf16[256,512]{1,0:T(8,128)(2,1)} %shard_map.73, bf16[512,4096]{1,0:T(8,128)(2,1)} %param.13), kind=kOutput, calls=%fused_computation.2 | convolution fusion | flops 1074790400 | bytes 6553600 | tf_op jit(solution)/shard_map/dot_general | solution.py:165
  81.5 0.0 reduce-scatter.2.cloned.1.call-update
  81.5 80.9 %reduce-scatter.2.cloned.1.call-done = bf16[256,512]{1,0:T(8,128)(2,1)} async-done(((bf16[256,4096]{1,0:T(8,128)(2,1)}), bf16[256,512]{1,0:T(8,128)(2,1)}) %reduce-scatter.2.cloned.1.call-update) | async-done | bytes 262160 | tf_op jit(solution)/shard_map/reduce_scatter | solution.py:166
  (4 shorter events, 0.0 us)
Async XLA Ops:
  6.5 4.7 %copy-start = (bf16[4096,128]{1,0:T(8,128)(2,1)S(1)}, bf16[4096,128]{1,0:T(8,128)(2,1)}, u32[]{:S(2)}) copy-start(bf16[4096,128]{1,0:T(8,128)(2,1)} %param.11) | copy-start | bytes 3145732
  6.5 7.1 %copy-start.1 = (bf16[256,4096]{1,0:T(8,128)(2,1)S(1)}, bf16[256,4096]{1,0:T(8,128)(2,1)}, u32[]{:S(2)}) copy-start(bf16[256,4096]{1,0:T(8,128)(2,1)} %param.7) | copy-start | bytes 6291460
  6.5 61.4 %all-gather.2.cloned.1.call-start = ((), (), s32[]{:S(2)}) async-start(), calls=%async_computation.1 | async-start | bytes 4325376 | tf_op jit(solution)/shard_map/all_gather | solution.py:154
  7.7 6.0 %copy-start.2 = (bf16[4096,128]{1,0:T(8,128)(2,1)S(1)}, bf16[4096,128]{1,0:T(8,128)(2,1)}, u32[]{:S(2)}) copy-start(bf16[4096,128]{1,0:T(8,128)(2,1)} %param.12) | copy-start | bytes 3145732
  16.0 146.3 %reduce-scatter.2.cloned.1.call-start = ((), (), s32[]{:S(2)}) async-start(), calls=%async_computation.2 | async-start | bytes 2359296 | tf_op jit(solution)/shard_map/reduce_scatter | solution.py:166
Sparse Core Ops, SparseCore 0:
  16.1 51.8 all-gather.1
  81.6 80.7 reduce-scatter.1
